TPU v7x, 256 devices: a whole 4x4x8 slice. The times are simulated.
256 devices in a mesh: space: 32 (over z_hi, x, core), scen: 8 (over y, z_lo).
Axes of the slice: x: 4, y: 4, z: 8 (z_hi: 4, z_lo: 2; z = z_hi * 2 + z_lo), core: 2. Of those that a mesh axis runs over, the one named last changes fastest.
Arguments:
- concentration: float32 [8, 8, 6, 384, 384], P('scen', None, None, 'space'), may hold values from -6 to 6
- emissions: float32 [8, 6, 384, 384], P('scen', None, 'space'), may hold values from -3 to 3
- courant: float32 [2, 8, 6, 384, 384], P(None, None, None, 'space'), may hold values from -0.9 to 0.9
- tile_source: int32 [8640], P('space'), may hold values from 0 to 215, as said below
- tile_target: int32 [8640], P('space'), may hold values from 0 to 1023, as said below
- intersection: bfloat16 [8640, 128, 128], P('space'), may hold values from 0 to 0.0625
Outputs:
- transported: float32 [8, 8, 6, 384, 384], P('scen', None, None, 'space')
- regridded: float32 [8, 8, 1024, 128], P('scen', None, 'space')
- ensemble_moments: float32 [2, 8, 1024, 128], P(None, None, 'space')
Inputs may be any that keep to these rules, and one draw needn't show every extreme that they name: `tile_source`: every source block of a row band is named by at least one of the band's tiles. `tile_target`: latitude band b holds target blocks b * 32 to (b+1) * 32 - 1. The 270 tiles of one row band name at most 16 blocks of any one latitude band and at least 8 of every latitude band but one, which receives exactly 16 tiles from every row band. Every target block is named by some tile.
All inputs are finite; a program needn't handle non-finite values.
Results may differ from a plain program's by a relative error of at most 0.0027.
Values sent between devices are 32-bit elements; how exact they have to be, the bound alone decides.
No kernel may reach another device: no remote copies, remote signals or barrier semaphores. Data moves between devices by JAX's collectives and lax.ppermute only.
A program may use at most 128 MiB of HBM per device.

v0:
```python
import jax
import jax.numpy as jnp
from jax import lax
from jax.sharding import PartitionSpec as P

TGT_DEV = 32
SLOTS = 16


def from_behind(block, axis, distance):
    devices = range(lax.axis_size(axis))
    route = [((i - distance) % len(devices), i) for i in devices]
    return lax.ppermute(block, axis, route)


def parabola_sweep(padded, courant_faces, sweep_axis):
    cells_along = padded.shape[sweep_axis] - 6

    def window(values_in, first_cell, length):
        return lax.slice_in_dim(values_in, first_cell, first_cell + length, axis=sweep_axis)

    edge_values = 7.0 / 12.0 * (
        window(padded, 1, cells_along + 3) + window(padded, 2, cells_along + 3)
    ) - 1.0 / 12.0 * (window(padded, 0, cells_along + 3) + window(padded, 3, cells_along + 3))
    left_edge = window(edge_values, 0, cells_along + 2)
    right_edge = window(edge_values, 1, cells_along + 2)
    centre = window(padded, 2, cells_along + 2)
    slopes = right_edge - left_edge
    curvature = 6.0 * centre - 3.0 * (left_edge + right_edge)
    backward = -courant_faces
    upwind_left = courant_faces * (
        window(right_edge, 0, cells_along + 1)
        - 0.5
        * courant_faces
        * (
            window(slopes, 0, cells_along + 1)
            - (1.0 - 2.0 * courant_faces / 3.0) * window(curvature, 0, cells_along + 1)
        )
    )
    upwind_right = courant_faces * (
        window(left_edge, 1, cells_along + 1)
        + 0.5
        * backward
        * (
            window(slopes, 1, cells_along + 1)
            + (1.0 - 2.0 * backward / 3.0) * window(curvature, 1, cells_along + 1)
        )
    )
    fluxes = jnp.where(courant_faces >= 0.0, upwind_left, upwind_right)
    return window(padded, 3, cells_along) - (
        window(fluxes, 1, cells_along) - window(fluxes, 0, cells_along)
    )


def by_destination(values, band_count):
    width = values.shape[-1]
    blocks = values.reshape(values.shape[:-1] + (band_count, width // band_count))
    return jnp.flip(jnp.moveaxis(blocks, -2, 0), 0).reshape(band_count, -1)


def pack_rows(tracer, north_wind, lowest):
    row_count = tracer.shape[3]
    width_cells = tracer.shape[4]
    if lowest:
        layers = tracer[:, :, :, 0:3, :]
    else:
        layers = tracer[:, :, :, row_count - 3 :, :]
    parts = [layers.reshape(-1, width_cells)]
    if north_wind is not None:
        wind_row = north_wind[:, :, 0:1, :] if lowest else north_wind[:, :, row_count - 1 :, :]
        parts.append(wind_row.reshape(-1, width_cells))
    return jnp.concatenate(parts, 0)


def edge_rows(tracer, north_wind, position, band_count, with_wind):
    row_count = tracer.shape[3]
    top_parts = [by_destination(tracer[:, :, 0::2, row_count - 3 :, :], band_count)]
    low_parts = [by_destination(tracer[:, :, 1::2, 0:3, :], band_count)]
    if with_wind:
        top_parts.append(by_destination(north_wind[:, 0::2, row_count - 1, :], band_count))
        low_parts.append(by_destination(north_wind[:, 1::2, 0, :], band_count))
    send_top = jnp.concatenate(top_parts, 1)
    send_low = jnp.concatenate(low_parts, 1)
    send = jnp.where(
        position == band_count - 1, send_top, jnp.where(position == 0, send_low, 0.0)
    ).astype(send_top.dtype)
    got = lax.all_to_all(send, "space", 0, 0, tiled=True)
    return (got[band_count - 1], got[0])


def column_halos(tracer, east_wind, north_wind, position, band_count, edge_wind):
    scenarios, levels, _, row_count, width_cells = tracer.shape
    top, low = edge_rows(tracer, north_wind, position, band_count, edge_wind is None)
    cells = scenarios * levels * 3 * 3 * row_count
    top_layers = top[:cells].reshape(scenarios, levels, 3, 3, row_count)
    low_layers = low[:cells].reshape(scenarios, levels, 3, 3, row_count)
    if edge_wind is None:
        edge_wind = (
            top[cells:].reshape(levels, 3, row_count),
            low[cells:].reshape(levels, 3, row_count),
        )
    top_wind, low_wind = edge_wind
    padded_faces = []
    speed_faces = []
    for face_number in range(6):
        half = face_number // 2
        if face_number % 2 == 0:
            source = top_layers[:, :, (half - 1) % 3]
            west_cells = jnp.swapaxes(jnp.flip(source, -1), -1, -2)
            west_speed = jnp.flip(top_wind[:, (half - 1) % 3], -1)
            east_cells = tracer[:, :, (face_number + 1) % 6, :, 0:3]
            east_speed = east_wind[:, (face_number + 1) % 6, :, 0]
        else:
            west_cells = tracer[:, :, (face_number - 1) % 6, :, width_cells - 3 :]
            west_speed = east_wind[:, (face_number - 1) % 6, :, width_cells - 1]
            source = low_layers[:, :, (half + 1) % 3]
            east_cells = jnp.swapaxes(jnp.flip(source, -1), -1, -2)
            east_speed = jnp.flip(low_wind[:, (half + 1) % 3], -1)
        padded_faces.append(
            jnp.concatenate([west_cells, tracer[:, :, face_number], east_cells], -1)
        )
        speeds = jnp.concatenate(
            [west_speed[:, :, None], east_wind[:, face_number], east_speed[:, :, None]], -1
        )
        speed_faces.append(0.5 * (speeds[:, :, :-1] + speeds[:, :, 1:]))
    return (jnp.stack(padded_faces, 2), jnp.stack(speed_faces, 1), edge_wind)


def edge_columns(tracer, east_wind, position, band_count, with_wind):
    scenarios, levels, _, row_count, width_cells = tracer.shape
    to_top = [jnp.swapaxes(tracer[:, :, 0::2, :, 0:3], -1, -2).reshape(-1)]
    to_low = [jnp.swapaxes(tracer[:, :, 1::2, :, width_cells - 3 :], -1, -2).reshape(-1)]
    if with_wind:
        to_top.append(east_wind[:, 0::2, :, 0].reshape(-1))
        to_low.append(east_wind[:, 1::2, :, width_cells - 1].reshape(-1))
    to_top = jnp.concatenate(to_top)
    to_low = jnp.concatenate(to_low)
    send = jnp.zeros((band_count,) + to_top.shape, to_top.dtype)
    send = send.at[band_count - 1].set(to_top).at[0].set(to_low)
    got = lax.all_to_all(send, "space", 0, 0, tiled=True)
    cells = scenarios * levels * 3 * 3 * row_count
    layers = got[:, :cells].reshape(band_count, scenarios, levels, 3, 3, row_count)
    layers = jnp.moveaxis(layers, 0, -2).reshape(scenarios, levels, 3, 3, band_count * row_count)
    wind = None
    if with_wind:
        wind = got[:, cells:].reshape(band_count, levels, 3, row_count)
        wind = jnp.moveaxis(wind, 0, -2).reshape(levels, 3, band_count * row_count)
    return (layers, wind)


def row_halos(tracer, east_wind, north_wind, position, band_count, row_wind):
    first_step = row_wind is None
    shifted = []
    for step_by, lowest in ((-1, True), (1, False)):
        packed = pack_rows(tracer, north_wind if first_step else None, lowest)
        shifted.append(from_behind(packed, "space", step_by))
    edge_layers, edge_speed = edge_columns(tracer, east_wind, position, band_count, first_step)
    layer_rows = tracer.shape[0] * tracer.shape[1] * 18
    width_cells = tracer.shape[4]
    if first_step:
        levels = tracer.shape[1]
        row_wind = tuple(
            (packed[layer_rows:].reshape(levels, 6, width_cells) for packed in shifted)
        ) + (edge_speed,)
    above_wind, below_wind, edge_speed = row_wind
    above_layers, below_layers = (
        packed[:layer_rows].reshape(tracer.shape[0], tracer.shape[1], 6, 3, width_cells)
        for packed in shifted
    )
    at_top = position == band_count - 1
    at_bottom = position == 0
    padded_faces = []
    speed_faces = []
    for face_number in range(6):
        half = face_number // 2
        if face_number % 2 == 0:
            north_cells = jnp.where(
                at_top,
                jnp.flip(edge_layers[:, :, (half + 1) % 3], -1),
                above_layers[:, :, face_number],
            )
            north_speed = jnp.where(
                at_top, jnp.flip(edge_speed[:, (half + 1) % 3], -1), above_wind[:, face_number]
            )
            south_cells = jnp.where(
                at_bottom,
                below_layers[:, :, (face_number - 1) % 6],
                below_layers[:, :, face_number],
            )
            south_speed = jnp.where(
                at_bottom, below_wind[:, (face_number - 1) % 6], below_wind[:, face_number]
            )
        else:
            north_cells = jnp.where(
                at_top, above_layers[:, :, (face_number + 1) % 6], above_layers[:, :, face_number]
            )
            north_speed = jnp.where(
                at_top, above_wind[:, (face_number + 1) % 6], above_wind[:, face_number]
            )
            south_cells = jnp.where(
                at_bottom,
                jnp.flip(edge_layers[:, :, (half - 1) % 3], -1),
                below_layers[:, :, face_number],
            )
            south_speed = jnp.where(
                at_bottom, jnp.flip(edge_speed[:, (half - 1) % 3], -1), below_wind[:, face_number]
            )
        padded_faces.append(
            jnp.concatenate([south_cells, tracer[:, :, face_number], north_cells], -2)
        )
        speeds = jnp.concatenate(
            [south_speed[:, None, :], north_wind[:, face_number], north_speed[:, None, :]], -2
        )
        speed_faces.append(0.5 * (speeds[:, :-1, :] + speeds[:, 1:, :]))
    return (jnp.stack(padded_faces, 2), jnp.stack(speed_faces, 1), row_wind)


def regrid(tracer, tile_source, tile_target, intersection, band_count):
    scenarios = tracer.shape[0]
    levels = tracer.shape[1]
    batch_rows = scenarios * levels
    block_cells = intersection.shape[1]
    blocks = tracer.astype(jnp.bfloat16).reshape(batch_rows, -1, block_cells)
    chosen = jnp.take(blocks, tile_source, axis=1)
    partial_value = jnp.einsum(
        "btk,tkc->tbc", chosen, intersection, preferred_element_type=jnp.float32
    )
    target_band = tile_target // TGT_DEV
    target_block = tile_target % TGT_DEV
    band_hot = (target_band[:, None] == jnp.arange(band_count)[None, :]).astype(jnp.int32)
    rank = jnp.sum((jnp.cumsum(band_hot, 0) - band_hot) * band_hot, 1)
    slot = jnp.where(rank < SLOTS, target_band * SLOTS + rank, -1)
    slot_hot = (slot[None, :] == jnp.arange(band_count * SLOTS)[:, None]).astype(jnp.float32)
    slotted = jnp.einsum("st,tbc->sbc", slot_hot, partial_value, precision=lax.Precision.HIGHEST)
    slot_block = jnp.sum(slot_hot * target_block[None, :].astype(jnp.float32), 1)
    index_rows = jnp.zeros((band_count, 8, block_cells), jnp.float32)
    index_rows = index_rows.at[:, 0, :SLOTS].set(slot_block.reshape(band_count, SLOTS))
    send = jnp.concatenate(
        [slotted.reshape(band_count, SLOTS * batch_rows, block_cells), index_rows], 1
    )
    got = lax.all_to_all(send, "space", 0, 0, tiled=True)
    values = got[:, : SLOTS * batch_rows].reshape(band_count * SLOTS, batch_rows, block_cells)
    got_block = got[:, SLOTS * batch_rows, :SLOTS].reshape(-1)
    block_hot = (got_block[None, :] == jnp.arange(TGT_DEV)[:, None].astype(jnp.float32)).astype(
        jnp.float32
    )
    summed = jnp.einsum("ks,sbc->bkc", block_hot, values, precision=lax.Precision.HIGHEST)
    return summed.reshape(scenarios, levels, TGT_DEV, block_cells)


def local(concentration, emissions, courant, tile_source, tile_target, intersection):
    band_count = lax.axis_size("space")
    position = lax.axis_index("space")
    tracer = concentration.at[:, 0].add(emissions)
    east_wind = courant[0]
    north_wind = courant[1]
    edge_wind = None
    row_wind = None
    for step_number in range(2):
        padded, courant_faces, edge_wind = column_halos(
            tracer, east_wind, north_wind, position, band_count, edge_wind
        )
        tracer = parabola_sweep(padded, courant_faces, 4)
        padded, courant_faces, row_wind = row_halos(
            tracer, east_wind, north_wind, position, band_count, row_wind
        )
        tracer = parabola_sweep(padded, courant_faces, 3)
    regridded = regrid(tracer, tile_source, tile_target, intersection, band_count)
    scenarios = tracer.shape[0]
    everyone = lax.all_gather(regridded, "scen", axis=0, tiled=True)
    moment_sums = jnp.stack([jnp.sum(everyone, 0), jnp.sum(everyone * everyone, 0)])
    ensemble_moments = moment_sums / (scenarios * lax.axis_size("scen"))
    return (tracer, regridded, ensemble_moments)


def solution(mesh):
    return jax.shard_map(
        local,
        mesh=mesh,
        in_specs=(
            P("scen", None, None, "space", None),
            P("scen", None, "space", None),
            P(None, None, None, "space", None),
            P("space"),
            P("space"),
            P("space", None, None),
        ),
        out_specs=(
            P("scen", None, None, "space", None),
            P("scen", None, "space", None),
            P(None, None, "space", None),
        ),
        check_vma=False,
    )
```

profile of v0, /device:TPU:2, one launch (start us, length us, event | category | flops | bytes accessed | tf_op | source)
XLA Modules:
  0.0 335.2 jit_solution(12581908648371963601)
XLA Ops:
  7.2 1.2 copy.746
  8.5 1.1 scatter-add.4
  9.6 1.3 reshape.3059
  12.7 1.3 reshape.3058
  15.1 1.2 copy.502
  16.3 1.5 slice_bitcast_fusion.1
  19.9 1.2 reshape_squeeze.18
  21.5 1.0 maximum_select_fusion
  23.3 12.0 %all-to-all-start = ((f32[32,1,1152]{2,1,0:T(1,128)}), f32[32,1,1152]{2,1,0:T(1,128)S(1)}, u32[]{:S(2)}, u32[]{:S(2)}) async-start(f32[32,1,1152]{2,1,0:T(1,128)} %copy.508), calls=%async_computation | async-start | bytes 294912 | tf_op jit(solution)/shard_map/all_to_all | solution.py:87
  48.1 0.9 bitcast_dynamic-update-slice_fusion.5
  58.4 1.5 copy.511
  60.7 1.1 fusion.80
  61.8 1.1 fusion.81
  62.9 1.1 fusion.82
  64.5 1.0 fusion.26
  67.8 1.2 fusion.19
  71.1 1.8 copy.527
  73.9 1.8 copy.525
  77.3 1.4 scatter.19
  78.7 1.7 copy.530
  80.4 9.8 %all-to-all-start.1 = ((f32[32,1,1152]{2,1,0:T(1,128)}), f32[32,1,1152]{2,1,0:T(1,128)}, u32[]{:S(2)}, u32[]{:S(2)}) async-start(f32[32,1,1152]{2,1,0:T(1,128)} %copy.530), calls=%async_computation.1 | async-start | bytes 294912 | tf_op jit(solution)/shard_map/all_to_all | solution.py:140
  90.3 1.7 copy.521
  92.0 1.8 reshape.3064
  93.8 1.7 copy.534
  95.5 1.8 reshape.3072
  97.2 1.7 pad_maximum_fusion.1
  99.1 1.7 pad_maximum_fusion
  103.5 1.0 copy.531
  104.5 1.1 reshape.3070
  105.6 1.5 copy.624
  107.1 2.1 reshape.3108
  110.5 1.3 rev.147
  112.3 1.6 rev.144
  114.0 2.2 rev.143
  116.2 1.4 rev.142
  123.3 0.9 slice.1208
  125.6 0.9 slice.1200
  132.8 3.2 reshape.3080
  136.0 3.0 rev.149
  139.1 3.2 reshape.3079
  142.3 3.0 rev.148
  145.3 1.3 select_select_fusion
  146.6 2.3 copy.573
  148.9 1.8 copy.574
  150.7 14.9 %all-to-all-start.2 = ((f32[32,1,864]{2,1,0:T(1,128)}), f32[32,1,864]{2,1,0:T(1,128)}, u32[]{:S(2)}, u32[]{:S(2)}) async-start(f32[32,1,864]{2,1,0:T(1,128)} %copy.574), calls=%async_computation.2 | async-start | bytes 229376 | tf_op jit(solution)/shard_map/all_to_all | solution.py:87
  166.4 8.3 %all-to-all-done.2 = f32[32,1,864]{2,1,0:T(1,128)} async-done(((f32[32,1,864]{2,1,0:T(1,128)}), f32[32,1,864]{2,1,0:T(1,128)}, u32[]{:S(2)}, u32[]{:S(2)}) %all-to-all-start.2) | async-done | bytes 110624 | tf_op jit(solution)/shard_map/all_to_all | solution.py:87
  178.4 1.1 fusion.92
  181.0 1.0 fusion.13
  182.7 1.2 fusion.6
  186.2 5.2 %all-to-all-start.3 = ((f32[32,1,864]{2,1,0:T(1,128)}), f32[32,1,864]{2,1,0:T(1,128)S(1)}, u32[]{:S(2)}, u32[]{:S(2)}) async-start(f32[32,1,864]{2,1,0:T(1,128)} %copy.587), calls=%async_computation.3 | async-start | bytes 229376 | tf_op jit(solution)/shard_map/all_to_all | solution.py:140
  192.0 1.9 collective-permute-start.3
  193.9 7.1 %all-to-all-done.3 = f32[32,1,864]{2,1,0:T(1,128)S(1)} async-done(((f32[32,1,864]{2,1,0:T(1,128)}), f32[32,1,864]{2,1,0:T(1,128)S(1)}, u32[]{:S(2)}, u32[]{:S(2)}) %all-to-all-start.3) | async-done | bytes 110624 | tf_op jit(solution)/shard_map/all_to_all | solution.py:140
  205.3 1.0 copy-done.2
  207.2 1.1 fusion.150
  208.3 1.8 gather_fusion
  210.1 4.9 %fusion.62 = f32[270,8,128]{2,1,0:T(8,128)S(1)} fusion(bf16[270,128,128]{2,1,0:T(8,128)(2,1)} %param.23, bf16[270,8,128]{2,1,0:T(8,128)(2,1)S(1)} %gather_fusion, pred[270]{0:T(512)(128)(4,1)S(1)} %copy-done.61), kind=kOutput, calls=%fused_computation.103 | convolution fusion | flops 71055360 | bytes 10506510 | tf_op jit(solution)/shard_map/btk,tkc->tbc/dot_general | solution.py:225
  215.0 2.0 fusion.28
  217.1 1.2 copy.621
  218.3 1.5 select_maximum_fusion
  219.8 9.5 %all-to-all-start.4 = ((f32[32,136,128]{2,1,0:T(8,128)}), f32[32,136,128]{2,1,0:T(8,128)S(1)}, u32[]{:S(2)}, u32[]{:S(2)}) async-start(f32[32,136,128]{2,1,0:T(8,128)} %select_maximum_fusion), calls=%async_computation.4 | async-start | bytes 4456448 | tf_op jit(solution)/shard_map/all_to_all | solution.py:241
  229.4 52.0 %all-to-all-done.4 = f32[32,136,128]{2,1,0:T(8,128)S(1)} async-done(((f32[32,136,128]{2,1,0:T(8,128)}), f32[32,136,128]{2,1,0:T(8,128)S(1)}, u32[]{:S(2)}, u32[]{:S(2)}) %all-to-all-start.4) | async-done | bytes 2228256 | tf_op jit(solution)/shard_map/all_to_all | solution.py:241
  281.8 1.7 fusion
  283.5 42.5 %all-gather.3.cloned.1.call-done = f32[64,32,128]{2,1,0:T(8,128)} async-done(((f32[8,32,128]{2,1,0:T(8,128)}), f32[64,32,128]{2,1,0:T(8,128)}) %all-gather.3.cloned.1.call-update) | async-done | bytes 1048592 | tf_op jit(solution)/shard_map/all_gather | solution.py:270
  326.0 1.4 fusion.149
  (384 shorter events, 69.2 us)
Async XLA Ops:
  7.2 1.2 copy-start.45
  21.1 14.2 %copy-start.60 = (s32[270]{0:T(512)S(1)}, s32[270]{0:T(512)}, u32[]{:S(2)}) copy-start(s32[270]{0:T(512)} %param.21) | copy-start | bytes 3244
  23.3 22.2 %all-to-all-start = ((f32[32,1,1152]{2,1,0:T(1,128)}), f32[32,1,1152]{2,1,0:T(1,128)S(1)}, u32[]{:S(2)}, u32[]{:S(2)}) async-start(f32[32,1,1152]{2,1,0:T(1,128)} %copy.508), calls=%async_computation | async-start | bytes 294912 | tf_op jit(solution)/shard_map/all_to_all | solution.py:87
  39.8 1.4 copy-start.55
  58.4 5.9 %copy-start.16 = (f32[1,8,12,384]{3,1,2,0:T(8,128)S(1)}, f32[1,8,12,384]{3,1,2,0:T(8,128)}, u32[]{:S(2)}) copy-start(f32[1,8,12,384]{3,1,2,0:T(8,128)} %get-tuple-element.157) | copy-start | bytes 442372
  60.7 3.3 copy-start.18
  60.7 3.3 copy-start.35
  60.7 3.4 %copy-start.43 = (f32[1,8,12,3]{3,1,2,0:T(8,128)S(1)}, f32[1,8,12,3]{3,1,2,0:T(8,128)}, u32[]{:S(2)}) copy-start(f32[1,8,12,3]{3,1,2,0:T(8,128)} %copy.512) | copy-start | bytes 3460
  60.7 3.5 %copy-start.17 = (f32[1,8,12,384]{3,1,2,0:T(8,128)S(1)}, f32[1,8,12,384]{3,1,2,0:T(8,128)}, u32[]{:S(2)}) copy-start(f32[1,8,12,384]{3,1,2,0:T(8,128)} %get-tuple-element.158) | copy-start | bytes 442372
  60.7 3.5 %copy-start.34 = (f32[1,8,12,3]{3,1,2,0:T(8,128)S(1)}, f32[1,8,12,3]{3,1,2,0:T(8,128)}, u32[]{:S(2)}) copy-start(f32[1,8,12,3]{3,1,2,0:T(8,128)} %get-tuple-element.152) | copy-start | bytes 3460
  60.7 3.5 %copy-start.44 = (f32[1,8,12,3]{3,1,2,0:T(8,128)S(1)}, f32[1,8,12,3]{3,1,2,0:T(8,128)}, u32[]{:S(2)}) copy-start(f32[1,8,12,3]{3,1,2,0:T(8,128)} %copy.513) | copy-start | bytes 3460
  60.7 3.6 %copy-start.33 = (f32[1,8,12,3]{3,1,2,0:T(8,128)S(1)}, f32[1,8,12,3]{3,1,2,0:T(8,128)}, u32[]{:S(2)}) copy-start(f32[1,8,12,3]{3,1,2,0:T(8,128)} %get-tuple-element.151) | copy-start | bytes 3460
  60.7 3.6 %copy-start.42 = (f32[1,8,12,3]{3,1,2,0:T(8,128)S(1)}, f32[1,8,12,3]{3,1,2,0:T(8,128)}, u32[]{:S(2)}) copy-start(f32[1,8,12,3]{3,1,2,0:T(8,128)} %copy.514) | copy-start | bytes 3460
  64.5 1.0 copy-start.26
  64.5 1.0 copy-start.31
  64.5 1.3 copy-start.25
  64.5 1.3 copy-start.30
  65.7 0.9 copy-start.23
  69.5 4.3 %copy-start.59 = (f32[288]{0:T(512)S(1)}, f32[288]{0:T(512)}, u32[]{:S(2)}) copy-start(f32[288]{0:T(512)} %reshape_squeeze.21) | copy-start | bytes 3460
  69.5 7.0 %copy-start.58 = (f32[288]{0:T(512)S(1)}, f32[288]{0:T(512)}, u32[]{:S(2)}) copy-start(f32[288]{0:T(512)} %reshape_squeeze.20) | copy-start | bytes 3460
  80.4 22.2 %all-to-all-start.1 = ((f32[32,1,1152]{2,1,0:T(1,128)}), f32[32,1,1152]{2,1,0:T(1,128)}, u32[]{:S(2)}, u32[]{:S(2)}) async-start(f32[32,1,1152]{2,1,0:T(1,128)} %copy.530), calls=%async_computation.1 | async-start | bytes 294912 | tf_op jit(solution)/shard_map/all_to_all | solution.py:140
  99.0 18.6 %collective-permute-start.1 = (f32[192,384]{1,0:T(8,128)}, f32[192,384]{1,0:T(8,128)}, u32[]{:S(2)}, u32[]{:S(2)}) collective-permute-start(f32[192,384]{1,0:T(8,128)} %pad_maximum_fusion.1), channel_id=1, source_target_pairs={{8,0},{16,8},{24,16},{32,24},{40,32},{48,40},{56,48},{64,56},{72,6... | collective-permute-start | bytes 884744 | tf_op jit(solution)/shard_map/ppermute | solution.py:13
  100.8 18.4 %collective-permute-start = (f32[192,384]{1,0:T(8,128)}, f32[192,384]{1,0:T(8,128)}, u32[]{:S(2)}, u32[]{:S(2)}) collective-permute-start(f32[192,384]{1,0:T(8,128)} %pad_maximum_fusion), channel_id=1, source_target_pairs={{248,0},{0,8},{8,16},{16,24},{24,32},{32,40},{40,48},{48,56},{56,6... | collective-permute-start | bytes 884744 | tf_op jit(solution)/shard_map/ppermute | solution.py:13
  110.1 6.1 %copy-start.41 = (f32[1,8,3,384]{3,2,1,0:T(4,128)S(1)}, f32[1,8,3,384]{3,2,1,0:T(4,128)}, u32[]{:S(2)}) copy-start(f32[1,8,3,384]{3,2,1,0:T(4,128)} %get-tuple-element.196) | copy-start | bytes 110596
  110.1 11.3 %copy-start.9 = (f32[8,1,12,384]{3,0,2,1:T(8,128)S(1)}, f32[8,1,12,384]{3,0,2,1:T(8,128)}, u32[]{:S(2)}) copy-start(f32[8,1,12,384]{3,0,2,1:T(8,128)} %get-tuple-element.124) | copy-start | bytes 442372
  126.6 1.2 copy-start.3
  126.6 1.2 copy-start.8
  126.6 1.2 copy-start.47
  126.6 1.2 copy-start.50
  126.7 1.5 copy-start
  126.8 1.5 copy-start.7
  126.8 1.5 copy-start.49
  126.9 1.4 copy-start.52
  126.9 1.4 copy-start.53
  126.9 1.4 copy-start.54
  126.9 1.4 copy-start.6
  128.3 0.9 copy-start.15
  128.4 0.9 copy-start.14
  128.4 1.0 copy-start.13
  128.5 1.0 copy-start.12
  128.9 1.0 copy-start.11
  129.0 1.5 copy-start.4
  129.0 1.5 copy-start.1
  129.0 1.1 copy-start.10
  150.7 24.0 %all-to-all-start.2 = ((f32[32,1,864]{2,1,0:T(1,128)}), f32[32,1,864]{2,1,0:T(1,128)}, u32[]{:S(2)}, u32[]{:S(2)}) async-start(f32[32,1,864]{2,1,0:T(1,128)} %copy.574), calls=%async_computation.2 | async-start | bytes 229376 | tf_op jit(solution)/shard_map/all_to_all | solution.py:87
  166.4 13.1 %copy-start.21 = (f32[1,8,12,384]{3,1,2,0:T(8,128)S(1)}, f32[1,8,12,384]{3,1,2,0:T(8,128)}, u32[]{:S(2)}) copy-start(f32[1,8,12,384]{3,1,2,0:T(8,128)} %get-tuple-element.115) | copy-start | bytes 442372
  166.4 13.1 %copy-start.40 = (f32[1,8,12,3]{3,1,2,0:T(8,128)S(1)}, f32[1,8,12,3]{3,1,2,0:T(8,128)}, u32[]{:S(2)}) copy-start(f32[1,8,12,3]{3,1,2,0:T(8,128)} %get-tuple-element.109) | copy-start | bytes 3460
  166.4 13.3 %copy-start.20 = (f32[1,8,12,384]{3,1,2,0:T(8,128)S(1)}, f32[1,8,12,384]{3,1,2,0:T(8,128)}, u32[]{:S(2)}) copy-start(f32[1,8,12,384]{3,1,2,0:T(8,128)} %get-tuple-element.114) | copy-start | bytes 442372
  166.4 13.3 %copy-start.39 = (f32[1,8,12,3]{3,1,2,0:T(8,128)S(1)}, f32[1,8,12,3]{3,1,2,0:T(8,128)}, u32[]{:S(2)}) copy-start(f32[1,8,12,3]{3,1,2,0:T(8,128)} %get-tuple-element.108) | copy-start | bytes 3460
  166.4 14.2 %copy-start.19 = (f32[1,8,12,384]{3,1,2,0:T(8,128)S(1)}, f32[1,8,12,384]{3,1,2,0:T(8,128)}, u32[]{:S(2)}) copy-start(f32[1,8,12,384]{3,1,2,0:T(8,128)} %get-tuple-element.113) | copy-start | bytes 442372
  166.4 14.2 %copy-start.38 = (f32[1,8,12,3]{3,1,2,0:T(8,128)S(1)}, f32[1,8,12,3]{3,1,2,0:T(8,128)}, u32[]{:S(2)}) copy-start(f32[1,8,12,3]{3,1,2,0:T(8,128)} %get-tuple-element.107) | copy-start | bytes 3460
  176.0 4.7 %copy-start.37 = (f32[1,8,12,3]{3,1,2,0:T(8,128)S(1)}, f32[1,8,12,3]{3,1,2,0:T(8,128)}, u32[]{:S(2)}) copy-start(f32[1,8,12,3]{3,1,2,0:T(8,128)} %get-tuple-element.106) | copy-start | bytes 3460
  177.5 3.4 %copy-start.36 = (f32[1,8,12,3]{3,1,2,0:T(8,128)S(1)}, f32[1,8,12,3]{3,1,2,0:T(8,128)}, u32[]{:S(2)}) copy-start(f32[1,8,12,3]{3,1,2,0:T(8,128)} %get-tuple-element.105) | copy-start | bytes 3460
  186.2 14.8 %all-to-all-start.3 = ((f32[32,1,864]{2,1,0:T(1,128)}), f32[32,1,864]{2,1,0:T(1,128)S(1)}, u32[]{:S(2)}, u32[]{:S(2)}) async-start(f32[32,1,864]{2,1,0:T(1,128)} %copy.587), calls=%async_computation.3 | async-start | bytes 229376 | tf_op jit(solution)/shard_map/all_to_all | solution.py:140
  191.6 12.7 %collective-permute-start.2 = (f32[144,384]{1,0:T(8,128)S(1)}, f32[144,384]{1,0:T(8,128)S(1)}, u32[]{:S(2)}, u32[]{:S(2)}) collective-permute-start(f32[144,384]{1,0:T(8,128)S(1)} %reshape.3081), channel_id=1, source_target_pairs={{248,0},{0,8},{8,16},{16,24},{24,32},{32,40},{40,48},{48,56},{56,6... | collective-permute-start | bytes 663560 | tf_op jit(solution)/shard_map/ppermute | solution.py:13
  192.0 12.5 %collective-permute-start.3 = (f32[144,384]{1,0:T(8,128)S(1)}, f32[144,384]{1,0:T(8,128)S(1)}, u32[]{:S(2)}, u32[]{:S(2)}) collective-permute-start(f32[144,384]{1,0:T(8,128)S(1)} %reshape.3086), channel_id=1, source_target_pairs={{8,0},{16,8},{24,16},{32,24},{40,32},{48,40},{56,48},{64,56},{72,6... | collective-permute-start | bytes 663560 | tf_op jit(solution)/shard_map/ppermute | solution.py:13
  205.1 1.2 copy-start.2
  205.1 1.5 copy-start.5
  207.2 1.1 copy-start.57
  207.2 2.9 copy-start.61
  210.1 4.9 %copy-start.56 = (s32[270]{0:T(512)S(1)}, s32[270]{0:T(512)}, u32[]{:S(2)}) copy-start(s32[270]{0:T(512)} %copy-done.55) | copy-start | bytes 3244
  217.1 1.2 copy-start.51
  219.8 61.6 %all-to-all-start.4 = ((f32[32,136,128]{2,1,0:T(8,128)}), f32[32,136,128]{2,1,0:T(8,128)S(1)}, u32[]{:S(2)}, u32[]{:S(2)}) async-start(f32[32,136,128]{2,1,0:T(8,128)} %select_maximum_fusion), calls=%async_computation.4 | async-start | bytes 4456448 | tf_op jit(solution)/shard_map/all_to_all | solution.py:241
  229.3 96.7 %all-gather.3.cloned.1.call-start = ((), (), s32[]{:S(2)}) async-start(), calls=%async_computation.5 | async-start | bytes 1179648 | tf_op jit(solution)/shard_map/all_gather | solution.py:270
  (9 other events, 7.3 us)
Sparse Core Ops, SparseCore 0:
  283.6 42.3 all-gather.2
where the time goes:
time: 341 us; the launch traced here: 335 us
  local copies, waits for them, and re-layouts  110 us (32%)
  waiting for transfers between devices  110 us (32%)
  starting transfers between devices  54.6 us (16%)
  other arithmetic  36.2 us (11%)
  between operations  16.2 us (5%)
  matrix products  8.66 us (3%)
    all_to_all x1, waiting for transfers between devices, regrid(): got = lax.all_to_all(send, 'space', 0, 0, tiled=True)  52 us
    all_gather x1, waiting for transfers between devices, local(): everyone = lax.all_gather(regridded, 'scen', axis=0, tiled=True)  42.5 us
    all_to_all x2, starting transfers between devices, edge_rows(): got = lax.all_to_all(send, 'space', 0, 0, tiled=True)  26.9 us
    all_to_all x2, starting transfers between devices, edge_columns(): got = lax.all_to_all(send, 'space', 0, 0, tiled=True)  15 us
    unnamed x40, other arithmetic  10.3 us
    all_to_all x1, starting transfers between devices, regrid(): got = lax.all_to_all(send, 'space', 0, 0, tiled=True)  9.5 us
    reshape x4, local copies, waits for them, and re-layouts, by_destination(): values.reshape(values.shape[:-1] + (band_count, width // band_count))  8.99 us
    rev x10, local copies, waits for them, and re-layouts, by_destination(): return jnp.flip(jnp.moveaxis(blocks, -2, 0), 0).reshape(band_count, -1)  8.87 us
  transfers between devices with their start and end apart: 10, of which 4 were waited for; matrix products, arithmetic and copies ran while one was open for 13% of the time, Pallas kernels for 0%

commit v1 on v0

--- a/solution.py
+++ b/solution.py
@@ -267,7 +267,9 @@
         tracer = parabola_sweep(padded, courant_faces, 3)
     regridded = regrid(tracer, tile_source, tile_target, intersection, band_count)
     scenarios = tracer.shape[0]
-    everyone = lax.all_gather(regridded, "scen", axis=0, tiled=True)
+    everyone = jnp.concatenate(
+        lax.all_to_all(jnp.stack(lax.axis_size("scen") * [regridded], 0), "scen", 0, 0), 0
+    )
     moment_sums = jnp.stack([jnp.sum(everyone, 0), jnp.sum(everyone * everyone, 0)])
     ensemble_moments = moment_sums / (scenarios * lax.axis_size("scen"))
     return (tracer, regridded, ensemble_moments)

time: 341 us -> 306 us (0.90)
  the two profiles are of different devices: /device:TPU:2 before, /device:TPU:1 now
where the time goes in v1:
time: 306 us; the launch traced here: 300 us
  local copies, waits for them, and re-layouts  110 us (36%)
  waiting for transfers between devices  73.1 us (24%)
  starting transfers between devices  51.7 us (17%)
  other arithmetic  34.9 us (11%)
  blocking collectives  19.6 us (6%)
  matrix products  7.98 us (3%)
    all_to_all x1, waiting for transfers between devices, regrid(): got = lax.all_to_all(send, 'space', 0, 0, tiled=True)  53.8 us
    all_to_all x2, starting transfers between devices, edge_rows(): got = lax.all_to_all(send, 'space', 0, 0, tiled=True)  26.6 us
    all_to_all x1, blocking collectives, local(): lax.all_to_all(jnp.stack(lax.axis_size('scen') * [regridded], 0), 'scen',...  19.6 us
    all_to_all x2, starting transfers between devices, edge_columns(): got = lax.all_to_all(send, 'space', 0, 0, tiled=True)  12.5 us
    all_to_all x2, waiting for transfers between devices, edge_rows(): got = lax.all_to_all(send, 'space', 0, 0, tiled=True)  10.9 us
    unnamed x40, other arithmetic  10.4 us
    reshape x4, local copies, waits for them, and re-layouts, by_destination(): values.reshape(values.shape[:-1] + (band_count, width // band_count))  9.01 us
    rev x10, local copies, waits for them, and re-layouts, by_destination(): return jnp.flip(jnp.moveaxis(blocks, -2, 0), 0).reshape(band_count, -1)  8.9 us
  transfers between devices with their start and end apart: 9, of which 4 were waited for; matrix products, arithmetic and copies ran while one was open for 14% of the time, Pallas kernels for 0%

profile of v1, /device:TPU:1, one launch (start us, length us, event | category | flops | bytes accessed | tf_op | source)
XLA Modules:
  0.0 299.7 jit_solution(3051255712790396572)
XLA Ops:
  0.6 1.2 copy.746
  2.0 1.1 scatter-add.4
  3.1 1.3 reshape.3063
  6.1 1.3 reshape.3062
  8.6 1.2 copy.502
  9.7 1.5 slice_bitcast_fusion.1
  13.4 1.2 reshape_squeeze.18
  15.0 1.0 maximum_select_fusion
  16.8 13.0 %all-to-all-start = ((f32[32,1,1152]{2,1,0:T(1,128)}), f32[32,1,1152]{2,1,0:T(1,128)S(1)}, u32[]{:S(2)}, u32[]{:S(2)}) async-start(f32[32,1,1152]{2,1,0:T(1,128)} %copy.508), calls=%async_computation | async-start | bytes 294912 | tf_op jit(solution)/shard_map/all_to_all | solution.py:87
  39.8 1.1 all-to-all-done
  53.8 1.5 copy.511
  56.1 1.1 fusion.80
  57.2 1.1 fusion.81
  58.3 1.1 fusion.82
  59.9 1.0 fusion.26
  63.2 1.2 fusion.19
  66.5 1.8 copy.527
  69.2 1.8 copy.525
  72.7 1.4 scatter.19
  74.1 1.7 copy.530
  75.8 8.7 %all-to-all-start.1 = ((f32[32,1,1152]{2,1,0:T(1,128)}), f32[32,1,1152]{2,1,0:T(1,128)}, u32[]{:S(2)}, u32[]{:S(2)}) async-start(f32[32,1,1152]{2,1,0:T(1,128)} %copy.530), calls=%async_computation.1 | async-start | bytes 294912 | tf_op jit(solution)/shard_map/all_to_all | solution.py:140
  84.6 1.7 copy.521
  86.3 1.8 reshape.3068
  88.1 1.7 copy.534
  89.8 1.8 reshape.3076
  91.5 1.7 pad_maximum_fusion.1
  93.5 1.7 pad_maximum_fusion
  95.3 1.9 collective-permute-start
  99.1 1.0 copy.531
  100.0 1.1 reshape.3074
  101.1 1.5 copy.624
  102.6 2.1 reshape.3111
  106.1 1.3 rev.147
  107.8 1.6 rev.144
  109.5 2.2 rev.143
  111.7 1.4 rev.142
  118.8 0.9 slice.1208
  121.1 0.9 slice.1200
  128.3 3.2 %reshape.3084 = f32[1,8,3,3,32,12]{5,4,1,3,2,0:T(8,128)} reshape(f32[1,8,3,3,384]{4,1,3,2,0:T(8,128)} %get-tuple-element.117) | data formatting | bytes 221184 | tf_op jit(solution)/shard_map/reshape | solution.py:57
  131.5 3.1 %rev.149 = f32[32,1,8,3,3,12]{5,0,2,4,3,1:T(8,128)} reverse(f32[32,1,8,3,3,12]{5,0,2,4,3,1:T(8,128)} %bitcast.607), dimensions={0} | reverse | bytes 221184 | tf_op jit(solution)/shard_map/jit(_flip)/rev | solution.py:58
  134.6 3.2 %reshape.3083 = f32[1,8,3,3,32,12]{5,4,1,3,2,0:T(8,128)} reshape(f32[1,8,3,3,384]{4,1,3,2,0:T(8,128)} %get-tuple-element.118) | data formatting | bytes 221184 | tf_op jit(solution)/shard_map/reshape | solution.py:57
  137.8 3.1 %rev.148 = f32[32,1,8,3,3,12]{5,0,2,4,3,1:T(8,128)} reverse(f32[32,1,8,3,3,12]{5,0,2,4,3,1:T(8,128)} %bitcast.608), dimensions={0} | reverse | bytes 221184 | tf_op jit(solution)/shard_map/jit(_flip)/rev | solution.py:58
  140.9 1.3 select_select_fusion
  142.2 2.3 copy.573
  144.5 1.8 copy.574
  146.3 13.6 %all-to-all-start.2 = ((f32[32,1,864]{2,1,0:T(1,128)}), f32[32,1,864]{2,1,0:T(1,128)}, u32[]{:S(2)}, u32[]{:S(2)}) async-start(f32[32,1,864]{2,1,0:T(1,128)} %copy.574), calls=%async_computation.2 | async-start | bytes 229376 | tf_op jit(solution)/shard_map/all_to_all | solution.py:87
  160.7 9.8 %all-to-all-done.2 = f32[32,1,864]{2,1,0:T(1,128)} async-done(((f32[32,1,864]{2,1,0:T(1,128)}), f32[32,1,864]{2,1,0:T(1,128)}, u32[]{:S(2)}, u32[]{:S(2)}) %all-to-all-start.2) | async-done | bytes 110624 | tf_op jit(solution)/shard_map/all_to_all | solution.py:87
  174.2 1.1 fusion.92
  176.8 1.0 fusion.13
  178.5 1.2 fusion.6
  182.0 3.7 %all-to-all-start.3 = ((f32[32,1,864]{2,1,0:T(1,128)}), f32[32,1,864]{2,1,0:T(1,128)S(1)}, u32[]{:S(2)}, u32[]{:S(2)}) async-start(f32[32,1,864]{2,1,0:T(1,128)} %copy.587), calls=%async_computation.3 | async-start | bytes 229376 | tf_op jit(solution)/shard_map/all_to_all | solution.py:140
  185.9 1.7 collective-permute-start.2
  188.2 8.4 %all-to-all-done.3 = f32[32,1,864]{2,1,0:T(1,128)S(1)} async-done(((f32[32,1,864]{2,1,0:T(1,128)}), f32[32,1,864]{2,1,0:T(1,128)S(1)}, u32[]{:S(2)}, u32[]{:S(2)}) %all-to-all-start.3) | async-done | bytes 110624 | tf_op jit(solution)/shard_map/all_to_all | solution.py:140
  200.8 1.0 copy-done.2
  202.8 1.1 fusion.150
  203.8 1.8 gather_fusion
  205.6 4.9 %fusion.62 = f32[270,8,128]{2,1,0:T(8,128)S(1)} fusion(bf16[270,128,128]{2,1,0:T(8,128)(2,1)} %param.23, bf16[270,8,128]{2,1,0:T(8,128)(2,1)S(1)} %gather_fusion, pred[270]{0:T(512)(128)(4,1)S(1)} %copy-done.62), kind=kOutput, calls=%fused_computation.103 | convolution fusion | flops 71055360 | bytes 10506510 | tf_op jit(solution)/shard_map/btk,tkc->tbc/dot_general | solution.py:225
  210.6 2.0 fusion.28
  212.6 1.2 copy.621
  213.8 1.5 select_maximum_fusion
  215.3 8.3 %all-to-all-start.4 = ((f32[32,136,128]{2,1,0:T(8,128)}), f32[32,136,128]{2,1,0:T(8,128)S(1)}, u32[]{:S(2)}, u32[]{:S(2)}) async-start(f32[32,136,128]{2,1,0:T(8,128)} %select_maximum_fusion), calls=%async_computation.4 | async-start | bytes 4456448 | tf_op jit(solution)/shard_map/all_to_all | solution.py:241
  223.7 53.8 %all-to-all-done.4 = f32[32,136,128]{2,1,0:T(8,128)S(1)} async-done(((f32[32,136,128]{2,1,0:T(8,128)}), f32[32,136,128]{2,1,0:T(8,128)S(1)}, u32[]{:S(2)}, u32[]{:S(2)}) %all-to-all-start.4) | async-done | bytes 2228256 | tf_op jit(solution)/shard_map/all_to_all | solution.py:241
  277.9 1.0 fusion
  279.1 19.6 %all_to_all.53 = f32[8,1,8,32,128]{4,3,2,1,0:T(8,128)S(1)} all-to-all(f32[8,1,8,32,128]{4,3,2,1,0:T(8,128)S(1)} %stack.200), channel_id=1, replica_groups=mesh['space'=32,'scen'=8] {'scen'}, dimensions={0} | all-to-all | bytes 2097152 | tf_op jit(solution)/shard_map/all_to_all | solution.py:271
  (385 shorter events, 69.6 us)
Async XLA Ops:
  0.6 1.2 copy-start.46
  14.6 15.2 %copy-start.61 = (s32[270]{0:T(512)S(1)}, s32[270]{0:T(512)}, u32[]{:S(2)}) copy-start(s32[270]{0:T(512)} %param.21) | copy-start | bytes 3244
  16.8 24.1 %all-to-all-start = ((f32[32,1,1152]{2,1,0:T(1,128)}), f32[32,1,1152]{2,1,0:T(1,128)S(1)}, u32[]{:S(2)}, u32[]{:S(2)}) async-start(f32[32,1,1152]{2,1,0:T(1,128)} %copy.508), calls=%async_computation | async-start | bytes 294912 | tf_op jit(solution)/shard_map/all_to_all | solution.py:87
  34.2 1.4 copy-start.56
  53.8 5.9 %copy-start.16 = (f32[1,8,12,384]{3,1,2,0:T(8,128)S(1)}, f32[1,8,12,384]{3,1,2,0:T(8,128)}, u32[]{:S(2)}) copy-start(f32[1,8,12,384]{3,1,2,0:T(8,128)} %get-tuple-element.157) | copy-start | bytes 442372
  56.0 3.3 %copy-start.18 = (f32[1,8,12,384]{3,1,2,0:T(8,128)S(1)}, f32[1,8,12,384]{3,1,2,0:T(8,128)}, u32[]{:S(2)}) copy-start(f32[1,8,12,384]{3,1,2,0:T(8,128)} %get-tuple-element.159) | copy-start | bytes 442372
  56.0 3.3 %copy-start.36 = (f32[1,8,12,3]{3,1,2,0:T(8,128)S(1)}, f32[1,8,12,3]{3,1,2,0:T(8,128)}, u32[]{:S(2)}) copy-start(f32[1,8,12,3]{3,1,2,0:T(8,128)} %get-tuple-element.153) | copy-start | bytes 3460
  56.0 3.4 %copy-start.44 = (f32[1,8,12,3]{3,1,2,0:T(8,128)S(1)}, f32[1,8,12,3]{3,1,2,0:T(8,128)}, u32[]{:S(2)}) copy-start(f32[1,8,12,3]{3,1,2,0:T(8,128)} %copy.512) | copy-start | bytes 3460
  56.0 3.5 %copy-start.17 = (f32[1,8,12,384]{3,1,2,0:T(8,128)S(1)}, f32[1,8,12,384]{3,1,2,0:T(8,128)}, u32[]{:S(2)}) copy-start(f32[1,8,12,384]{3,1,2,0:T(8,128)} %get-tuple-element.158) | copy-start | bytes 442372
  56.1 3.5 %copy-start.35 = (f32[1,8,12,3]{3,1,2,0:T(8,128)S(1)}, f32[1,8,12,3]{3,1,2,0:T(8,128)}, u32[]{:S(2)}) copy-start(f32[1,8,12,3]{3,1,2,0:T(8,128)} %get-tuple-element.152) | copy-start | bytes 3460
  56.1 3.5 %copy-start.45 = (f32[1,8,12,3]{3,1,2,0:T(8,128)S(1)}, f32[1,8,12,3]{3,1,2,0:T(8,128)}, u32[]{:S(2)}) copy-start(f32[1,8,12,3]{3,1,2,0:T(8,128)} %copy.513) | copy-start | bytes 3460
  56.1 3.6 %copy-start.34 = (f32[1,8,12,3]{3,1,2,0:T(8,128)S(1)}, f32[1,8,12,3]{3,1,2,0:T(8,128)}, u32[]{:S(2)}) copy-start(f32[1,8,12,3]{3,1,2,0:T(8,128)} %get-tuple-element.151) | copy-start | bytes 3460
  56.1 3.6 %copy-start.43 = (f32[1,8,12,3]{3,1,2,0:T(8,128)S(1)}, f32[1,8,12,3]{3,1,2,0:T(8,128)}, u32[]{:S(2)}) copy-start(f32[1,8,12,3]{3,1,2,0:T(8,128)} %copy.514) | copy-start | bytes 3460
  59.9 1.0 copy-start.27
  59.9 1.0 copy-start.32
  59.9 1.3 copy-start.26
  59.9 1.3 copy-start.31
  61.1 0.9 copy-start.24
  64.9 4.3 %copy-start.60 = (f32[288]{0:T(512)S(1)}, f32[288]{0:T(512)}, u32[]{:S(2)}) copy-start(f32[288]{0:T(512)} %reshape_squeeze.21) | copy-start | bytes 3460
  64.9 7.0 %copy-start.59 = (f32[288]{0:T(512)S(1)}, f32[288]{0:T(512)}, u32[]{:S(2)}) copy-start(f32[288]{0:T(512)} %reshape_squeeze.20) | copy-start | bytes 3460
  75.8 22.3 %all-to-all-start.1 = ((f32[32,1,1152]{2,1,0:T(1,128)}), f32[32,1,1152]{2,1,0:T(1,128)}, u32[]{:S(2)}, u32[]{:S(2)}) async-start(f32[32,1,1152]{2,1,0:T(1,128)} %copy.530), calls=%async_computation.1 | async-start | bytes 294912 | tf_op jit(solution)/shard_map/all_to_all | solution.py:140
  93.2 19.9 %collective-permute-start.1 = (f32[192,384]{1,0:T(8,128)}, f32[192,384]{1,0:T(8,128)}, u32[]{:S(2)}, u32[]{:S(2)}) collective-permute-start(f32[192,384]{1,0:T(8,128)} %pad_maximum_fusion.1), channel_id=1, source_target_pairs={{8,0},{16,8},{24,16},{32,24},{40,32},{48,40},{56,48},{64,56},{72,6... | collective-permute-start | bytes 884744 | tf_op jit(solution)/shard_map/ppermute | solution.py:13
  95.3 19.4 %collective-permute-start = (f32[192,384]{1,0:T(8,128)}, f32[192,384]{1,0:T(8,128)}, u32[]{:S(2)}, u32[]{:S(2)}) collective-permute-start(f32[192,384]{1,0:T(8,128)} %pad_maximum_fusion), channel_id=1, source_target_pairs={{248,0},{0,8},{8,16},{16,24},{24,32},{32,40},{40,48},{48,56},{56,6... | collective-permute-start | bytes 884744 | tf_op jit(solution)/shard_map/ppermute | solution.py:13
  105.6 6.1 %copy-start.42 = (f32[1,8,3,384]{3,2,1,0:T(4,128)S(1)}, f32[1,8,3,384]{3,2,1,0:T(4,128)}, u32[]{:S(2)}) copy-start(f32[1,8,3,384]{3,2,1,0:T(4,128)} %get-tuple-element.196) | copy-start | bytes 110596
  105.6 11.2 %copy-start.9 = (f32[8,1,12,384]{3,0,2,1:T(8,128)S(1)}, f32[8,1,12,384]{3,0,2,1:T(8,128)}, u32[]{:S(2)}) copy-start(f32[8,1,12,384]{3,0,2,1:T(8,128)} %get-tuple-element.124) | copy-start | bytes 442372
  122.1 1.2 copy-start.3
  122.2 1.2 copy-start.8
  122.2 1.2 copy-start.48
  122.2 1.2 copy-start.51
  122.3 1.5 copy-start
  122.3 1.5 copy-start.7
  122.3 1.5 copy-start.50
  122.4 1.4 copy-start.53
  122.4 1.4 copy-start.54
  122.4 1.4 copy-start.55
  122.4 1.4 copy-start.6
  123.8 0.9 copy-start.15
  123.9 0.9 copy-start.14
  124.0 1.0 copy-start.13
  124.0 1.0 copy-start.12
  124.5 1.0 copy-start.11
  124.5 1.5 copy-start.4
  124.5 1.5 copy-start.1
  124.5 1.1 copy-start.10
  146.3 24.2 %all-to-all-start.2 = ((f32[32,1,864]{2,1,0:T(1,128)}), f32[32,1,864]{2,1,0:T(1,128)}, u32[]{:S(2)}, u32[]{:S(2)}) async-start(f32[32,1,864]{2,1,0:T(1,128)} %copy.574), calls=%async_computation.2 | async-start | bytes 229376 | tf_op jit(solution)/shard_map/all_to_all | solution.py:87
  160.7 14.6 %copy-start.21 = (f32[1,8,12,384]{3,1,2,0:T(8,128)S(1)}, f32[1,8,12,384]{3,1,2,0:T(8,128)}, u32[]{:S(2)}) copy-start(f32[1,8,12,384]{3,1,2,0:T(8,128)} %get-tuple-element.115) | copy-start | bytes 442372
  160.7 14.6 %copy-start.41 = (f32[1,8,12,3]{3,1,2,0:T(8,128)S(1)}, f32[1,8,12,3]{3,1,2,0:T(8,128)}, u32[]{:S(2)}) copy-start(f32[1,8,12,3]{3,1,2,0:T(8,128)} %get-tuple-element.109) | copy-start | bytes 3460
  160.7 14.7 %copy-start.20 = (f32[1,8,12,384]{3,1,2,0:T(8,128)S(1)}, f32[1,8,12,384]{3,1,2,0:T(8,128)}, u32[]{:S(2)}) copy-start(f32[1,8,12,384]{3,1,2,0:T(8,128)} %get-tuple-element.114) | copy-start | bytes 442372
  160.7 14.7 %copy-start.40 = (f32[1,8,12,3]{3,1,2,0:T(8,128)S(1)}, f32[1,8,12,3]{3,1,2,0:T(8,128)}, u32[]{:S(2)}) copy-start(f32[1,8,12,3]{3,1,2,0:T(8,128)} %get-tuple-element.108) | copy-start | bytes 3460
  160.7 15.6 %copy-start.19 = (f32[1,8,12,384]{3,1,2,0:T(8,128)S(1)}, f32[1,8,12,384]{3,1,2,0:T(8,128)}, u32[]{:S(2)}) copy-start(f32[1,8,12,384]{3,1,2,0:T(8,128)} %get-tuple-element.113) | copy-start | bytes 442372
  160.7 15.6 %copy-start.39 = (f32[1,8,12,3]{3,1,2,0:T(8,128)S(1)}, f32[1,8,12,3]{3,1,2,0:T(8,128)}, u32[]{:S(2)}) copy-start(f32[1,8,12,3]{3,1,2,0:T(8,128)} %get-tuple-element.107) | copy-start | bytes 3460
  171.8 4.7 %copy-start.38 = (f32[1,8,12,3]{3,1,2,0:T(8,128)S(1)}, f32[1,8,12,3]{3,1,2,0:T(8,128)}, u32[]{:S(2)}) copy-start(f32[1,8,12,3]{3,1,2,0:T(8,128)} %get-tuple-element.106) | copy-start | bytes 3460
  173.3 3.4 %copy-start.37 = (f32[1,8,12,3]{3,1,2,0:T(8,128)S(1)}, f32[1,8,12,3]{3,1,2,0:T(8,128)}, u32[]{:S(2)}) copy-start(f32[1,8,12,3]{3,1,2,0:T(8,128)} %get-tuple-element.105) | copy-start | bytes 3460
  182.0 14.6 %all-to-all-start.3 = ((f32[32,1,864]{2,1,0:T(1,128)}), f32[32,1,864]{2,1,0:T(1,128)S(1)}, u32[]{:S(2)}, u32[]{:S(2)}) async-start(f32[32,1,864]{2,1,0:T(1,128)} %copy.587), calls=%async_computation.3 | async-start | bytes 229376 | tf_op jit(solution)/shard_map/all_to_all | solution.py:140
  185.9 13.8 %collective-permute-start.2 = (f32[144,384]{1,0:T(8,128)S(1)}, f32[144,384]{1,0:T(8,128)S(1)}, u32[]{:S(2)}, u32[]{:S(2)}) collective-permute-start(f32[144,384]{1,0:T(8,128)S(1)} %reshape.3085), channel_id=1, source_target_pairs={{248,0},{0,8},{8,16},{16,24},{24,32},{32,40},{40,48},{48,56},{56,6... | collective-permute-start | bytes 663560 | tf_op jit(solution)/shard_map/ppermute | solution.py:13
  187.8 12.1 %collective-permute-start.3 = (f32[144,384]{1,0:T(8,128)S(1)}, f32[144,384]{1,0:T(8,128)S(1)}, u32[]{:S(2)}, u32[]{:S(2)}) collective-permute-start(f32[144,384]{1,0:T(8,128)S(1)} %reshape.3090), channel_id=1, source_target_pairs={{8,0},{16,8},{24,16},{32,24},{40,32},{48,40},{56,48},{64,56},{72,6... | collective-permute-start | bytes 663560 | tf_op jit(solution)/shard_map/ppermute | solution.py:13
  200.6 1.2 copy-start.2
  200.6 1.5 copy-start.5
  202.7 1.1 copy-start.58
  202.7 2.9 copy-start.62
  205.6 4.9 %copy-start.57 = (s32[270]{0:T(512)S(1)}, s32[270]{0:T(512)}, u32[]{:S(2)}) copy-start(s32[270]{0:T(512)} %copy-done.56) | copy-start | bytes 3244
  212.6 1.2 copy-start.52
  215.3 62.2 %all-to-all-start.4 = ((f32[32,136,128]{2,1,0:T(8,128)}), f32[32,136,128]{2,1,0:T(8,128)S(1)}, u32[]{:S(2)}, u32[]{:S(2)}) async-start(f32[32,136,128]{2,1,0:T(8,128)} %select_maximum_fusion), calls=%async_computation.4 | async-start | bytes 4456448 | tf_op jit(solution)/shard_map/all_to_all | solution.py:241
  278.9 19.7 %copy-start.22 = (f32[8,128,32]{1,2,0:T(8,128)}, f32[8,128,32]{1,2,0:T(8,128)S(1)}, u32[]{:S(2)}) copy-start(f32[8,128,32]{1,2,0:T(8,128)S(1)} %fusion) | copy-start | bytes 393220
  (9 other events, 7.3 us)
